TPU v7x, 512 devices: a whole 4x4x16 slice. The times are simulated.
512 devices in a mesh: take: 4 (over y), outer: 16 (over z), inner: 8 (over x, core).
Axes of the slice: x: 4, y: 4, z: 16, core: 2. Of those that a mesh axis runs over, the one named last changes fastest.
Arguments:
- frames: bfloat16 [16, 65536, 256], P('take', ('outer', 'inner')), may hold values from -6 to 6
- conv_weight: bfloat16 [3, 3, 256, 256], replicated, may hold values from -0.21875 to 0.21875
- conv_bias: float32 [3, 256], replicated, may hold values from -1 to 1
- dilations: int32 [3], replicated, may hold values from 1 to 64, as said below
- head_weight: bfloat16 [256, 128], replicated, may hold values from -0.375 to 0.375
- present: int32 [16, 65536], P('take', ('outer', 'inner')), may hold values 0 or 1
- frame_keep: float32 [16, 65536], P('take', ('outer', 'inner')), may hold values from 0.5 to 1
- channel_params: float32 [3, 64], replicated, may hold values from 0 to 2
- head_cotangent: bfloat16 [16, 65536, 128], P('take', ('outer', 'inner')), may hold values from -6 to 6
Outputs:
- filtered_mean: float32 [16, 64, 65536], P('take', None, ('outer', 'inner'))
- head_grad: float32 [256, 128], replicated
Inputs may be any that keep to these rules, and one draw needn't show every extreme that they name: `dilations`: every dilation is 1 to 64; some layer has exactly 64 and another exactly 1.
All inputs are finite; a program needn't handle non-finite values. No bound on the sum of `present` on one device may be relied on, other than what follows from the above.
Results may differ from a plain program's by a relative error of at most 0.0048.
Values may be sent and summed in bfloat16 or wider, within the bound.
No kernel may reach another device: no remote copies, remote signals or barrier semaphores. Data moves between devices by JAX's collectives and lax.ppermute only.
A program may use at most 64 MiB of HBM per device.

v0:
```python
import jax
import jax.numpy as jnp
from jax import lax
from jax.sharding import PartitionSpec as P

STATE = 64
LAYERS = 3
DMAX = 64


def extended_2(block, sides, width):
    for axis, dim in sides:
        count = lax.axis_size(axis)
        forward = [(i, i + 1) for i in range(count - 1)]
        backward = [(target, source) for source, target in forward]
        low = lax.ppermute(
            lax.slice_in_dim(block, block.shape[dim] - width, None, axis=dim), axis, forward
        )
        high = lax.ppermute(lax.slice_in_dim(block, 0, width, axis=dim), axis, backward)
        block = jnp.concatenate([low, block, high], axis=dim)
    return block


def prefix_2(part, axis, combine, identity):
    place = lax.axis_index(axis)
    gathered = jax.tree.map(lambda a: lax.all_gather(a, axis), part)
    state = jax.tree.map(lambda a, e: jnp.zeros_like(a) + jnp.asarray(e, a.dtype), part, identity)

    def one(turn, state):
        return combine(
            state, jax.tree.map(lambda a: lax.dynamic_index_in_dim(a, turn, 0, False), gathered)
        )

    return lax.fori_loop(0, place, one, state)


def combine(early, late):
    a_one, b_one, c_one, e_one, j_one = early
    a_two, b_two, c_two, e_two, j_two = late
    denom = 1.0 + c_one * j_two
    new_a = a_two * a_one / denom
    new_b = a_two * (b_one + c_one * e_two) / denom + b_two
    new_c = a_two * a_two * c_one / denom + c_two
    new_e = a_one * (e_two - j_two * b_one) / denom + e_one
    new_j = a_one * a_one * j_two / denom + j_one
    return (new_a, new_b, new_c, new_e, new_j)


def doubling_prefix(elems, axis):
    length = elems[0].shape[axis]
    result = elems
    offset = 1
    while offset < length:
        moved = []
        for index, item in enumerate(result):
            fill_value = 1.0 if index == 0 else 0.0
            pad_shape = list(item.shape)
            pad_shape[axis] = offset
            fill = jnp.full(pad_shape, fill_value, item.dtype)
            kept = lax.slice_in_dim(item, 0, length - offset, axis=axis)
            moved.append(jnp.concatenate([fill, kept], axis=axis))
        result = combine(tuple(moved), result)
        offset = offset * 2
    return result


def exclusive_in_group(totals, axis):
    place = lax.axis_index(axis)
    gathered = lax.all_gather(totals, axis)
    inclusive = doubling_prefix(tuple((gathered[:, k] for k in range(5))), 0)
    inclusive = jnp.stack(inclusive, axis=1)
    earlier = lax.dynamic_index_in_dim(inclusive, jnp.maximum(place - 1, 0), 0, False)
    identity = jnp.zeros_like(earlier).at[0].set(1.0)
    earlier = jnp.where(place > 0, earlier, identity)
    return (earlier, inclusive[-1])


def block_prefix(totals):
    inner_excl, group_total = exclusive_in_group(totals, "inner")
    outer_excl, _ = exclusive_in_group(group_total, "outer")
    return combine(tuple(outer_excl), tuple(inner_excl))


def elements(obs, logp, params, present, keep, first):
    rate = params[0][:, None]
    noise = params[1][:, None]
    scale = params[2][:, None]
    trans = jnp.exp(-rate) * keep
    prec = present * scale * jax.nn.softplus(logp)
    denom = 1.0 + noise * prec
    zeros = jnp.zeros_like(obs)
    elem_a = jnp.where(first, zeros, trans / denom)
    elem_b = jnp.where(first, prec * obs / (1.0 + prec), noise * prec * obs / denom)
    elem_c = jnp.where(first, 1.0 / (1.0 + prec), noise / denom)
    elem_e = jnp.where(first, zeros, trans * prec * obs / denom)
    elem_j = jnp.where(first, zeros, trans * trans * prec / denom)
    return (elem_a, elem_b, elem_c, elem_e, elem_j)


def conv_layer(extended, weights, bias, dilation):
    out_len = extended.shape[1] - 2 * DMAX
    acc = jnp.zeros((extended.shape[0], out_len, extended.shape[2]), jnp.float32)
    for tap in range(3):
        piece = lax.dynamic_slice_in_dim(extended, DMAX + (tap - 1) * dilation, out_len, 1)
        acc = acc + jnp.einsum(
            "tfw,wv->tfv", piece, weights[tap], preferred_element_type=jnp.float32
        )
    center = extended[:, DMAX : DMAX + out_len]
    return (center.astype(jnp.float32) + jax.nn.silu(acc + bias[None, None, :])).astype(
        jnp.bfloat16
    )


def per_device(
    frames,
    conv_weight,
    conv_bias,
    dilations,
    head_weight,
    present,
    frame_keep,
    channel_params,
    head_cotangent,
):
    block_len = frames.shape[1]
    position = lax.axis_index(("outer", "inner"))
    hidden = frames
    for layer in range(LAYERS):
        extended = extended_2(hidden, ((("outer", "inner"), 1),), DMAX)
        hidden = conv_layer(extended, conv_weight[layer], conv_bias[layer], dilations[layer])
    head = jnp.einsum("tfw,ws->tsf", hidden, head_weight, preferred_element_type=jnp.float32)
    obs = head[:, :STATE]
    logp = head[:, STATE:]
    places = position * block_len + jnp.arange(block_len, dtype=jnp.int32)
    first = (places == 0)[None, None, :]
    elems = elements(
        obs,
        logp,
        channel_params,
        present.astype(jnp.float32)[:, None, :],
        frame_keep[:, None, :],
        first,
    )
    local = doubling_prefix(elems, 2)
    totals = jnp.stack([item[:, :, -1] for item in local])
    prefix = block_prefix(totals)
    final = combine(tuple((item[:, :, None] for item in prefix)), local)
    grad_local = jnp.einsum(
        "tfw,tfs->ws", hidden, head_cotangent, preferred_element_type=jnp.float32
    )
    head_grad = lax.psum(grad_local, "inner")
    head_grad = lax.psum(head_grad, "outer")
    head_grad = lax.psum(head_grad, "take")
    return (final[1], head_grad)


def solution(mesh):
    return jax.shard_map(
        per_device,
        mesh=mesh,
        in_specs=(
            P("take", ("outer", "inner"), None),
            P(),
            P(),
            P(),
            P(),
            P("take", ("outer", "inner")),
            P("take", ("outer", "inner")),
            P(),
            P("take", ("outer", "inner"), None),
        ),
        out_specs=(P("take", None, ("outer", "inner")), P()),
        check_vma=False,
    )
```

profile of v0, /device:TPU:2, one launch (start us, length us, event | category | flops | bytes accessed | tf_op | source)
XLA Modules:
  0.0 392.9 jit_solution(5290036489453492107)
XLA Ops:
  7.3 1.1 fusion.141
  8.4 1.9 collective-permute-start.1
  10.3 2.4 collective-permute-start
  12.7 0.8 exponential_bitcast_fusion
  13.5 0.8 fusion.142
  14.3 3.0 fusion.60
  17.3 0.7 fusion.143
  24.2 0.5 fusion.16
  24.7 1.1 copy-done.2
  25.8 1.1 add_convert_fusion.2
  26.9 3.0 collective-permute-start.2
  30.0 6.3 %collective-permute-start.3 = (bf16[4,64,256]{2,1,0:T(8,128)(2,1)S(1)}, bf16[4,64,256]{2,1,0:T(8,128)(2,1)S(1)}, u32[]{:S(2)}, u32[]{:S(2)}) collective-permute-start(bf16[4,64,256]{2,1,0:T(8,128)(2,1)S(1)} %get-tuple-element.108), channel_id=1, source_target_pairs={{1,0},{2,1},{3,2},{4,3},{5,4},{6,5},{7,6},{8,7},{9,8},{10,9},{11,1... | collective-permute-start | bytes 393224 | tf_op jit(solution)/shard_map/ppermute | solution.py:19
  36.3 0.4 fusion.56
  36.7 0.3 collective-permute-done.2
  37.0 1.8 collective-permute-done.3
  38.9 0.4 fusion.10
  39.3 1.1 add_convert_fusion.1
  40.5 1.9 collective-permute-start.4
  42.4 4.0 %collective-permute-start.5 = (bf16[4,64,256]{2,1,0:T(8,128)(2,1)S(1)}, bf16[4,64,256]{2,1,0:T(8,128)(2,1)S(1)}, u32[]{:S(2)}, u32[]{:S(2)}) collective-permute-start(bf16[4,64,256]{2,1,0:T(8,128)(2,1)S(1)} %get-tuple-element.106), channel_id=1, source_target_pairs={{1,0},{2,1},{3,2},{4,3},{5,4},{6,5},{7,6},{8,7},{9,8},{10,9},{11,1... | collective-permute-start | bytes 393224 | tf_op jit(solution)/shard_map/ppermute | solution.py:19
  46.4 0.4 fusion.52
  46.8 0.1 collective-permute-done.4
  46.9 1.8 collective-permute-done.5
  48.8 0.4 fusion.4
  49.2 1.1 add_convert_fusion
  50.4 0.5 convolution_bitcast_fusion
  50.9 0.4 divide_select_fusion.1
  51.3 0.8 divide_add_fusion.14
  52.2 1.1 divide_add_fusion.13
  53.3 1.3 divide_add_fusion.12
  54.6 1.3 divide_add_fusion.11
  55.9 1.3 divide_add_fusion.10
  57.2 1.3 divide_add_fusion.9
  58.5 1.3 divide_add_fusion.8
  59.9 1.4 fusion.30
  61.4 0.7 fusion.31
  62.2 0.4 fusion.34
  62.7 0.3 fusion.38
  63.0 0.2 slice_reduce_fusion.3
  63.2 0.4 fusion.50
  63.6 0.3 slice_reduce_fusion
  63.9 13.5 %all-gather = f32[40,4,64]{2,1,0:T(4,128)S(1)} all-gather(f32[5,4,64]{2,1,0:T(4,128)S(1)} %constant_dynamic-update-slice_fusion.3), channel_id=2, replica_groups=mesh['take'=4,'outer'=16,'inner'=8] {'inner'}, dimensions={0}, use_global_device_ids=true | all-gather | bytes 46080 | tf_op jit(solution)/shard_map/all_gather | solution.py:69
  77.9 38.7 %all_gather.11 = f32[16,5,4,64]{3,2,0,1:T(4,128)S(1)} all-gather(f32[1,5,4,64]{3,2,0,1:T(4,128)S(1)} %slice.674), channel_id=1, replica_groups=mesh['take'=4,'outer'=16,'inner'=8] {'outer'}, dimensions={0}, use_global_device_ids=true | all-gather | bytes 87040 | tf_op jit(solution)/shard_map/all_gather | solution.py:69
  116.8 1.1 convolution_bitcast_fusion.1
  118.5 69.9 %all-reduce.84.cloned.1.call-done = f32[256,128]{1,0:T(8,128)} async-done(((f32[256,128]{1,0:T(8,128)}), f32[256,128]{1,0:T(8,128)}) %all-reduce.84.cloned.1.call-update) | async-done | bytes 131088 | tf_op jit(solution)/shard_map/psum | solution.py:151
  188.6 139.9 %all-reduce.86.cloned.1.call-done = f32[256,128]{1,0:T(8,128)} async-done(((f32[256,128]{1,0:T(8,128)}), f32[256,128]{1,0:T(8,128)}) %all-reduce.86.cloned.1.call-update) | async-done | bytes 131088 | tf_op jit(solution)/shard_map/psum | solution.py:152
  328.5 1.0 divide_add_fusion
  329.6 55.2 %all-reduce.88.cloned.1.call-done = f32[256,128]{1,0:T(8,128)} async-done(((f32[256,128]{1,0:T(8,128)}), f32[256,128]{1,0:T(8,128)}) %all-reduce.88.cloned.1.call-update) | async-done | bytes 131088 | tf_op jit(solution)/shard_map/psum | solution.py:153
  384.8 1.6 copy.267
  (97 shorter events, 1.8 us)
Async XLA Ops:
  7.2 109.6 %copy-start = (bf16[4,512,128]{2,1,0:T(8,128)(2,1)S(1)}, bf16[4,512,128]{2,1,0:T(8,128)(2,1)}, u32[]{:S(2)}) copy-start(bf16[4,512,128]{2,1,0:T(8,128)(2,1)} %param.21) | copy-start | bytes 1572868
  7.2 16.9 %copy-start.1 = (bf16[4,512,256]{2,1,0:T(8,128)(2,1)S(1)}, bf16[4,512,256]{2,1,0:T(8,128)(2,1)}, u32[]{:S(2)}) copy-start(bf16[4,512,256]{2,1,0:T(8,128)(2,1)} %param.13) | copy-start | bytes 3145732
  7.2 10.1 %copy-start.8 = (s32[3]{0:T(128)S(1)}, s32[3]{0:T(128)}, u32[]{:S(2)}) copy-start(s32[3]{0:T(128)} %param.16) | copy-start | bytes 40
  7.2 16.8 %copy-start.7 = (s32[4,512]{1,0:T(4,128)S(1)}, s32[4,512]{1,0:T(4,128)}, u32[]{:S(2)}) copy-start(s32[4,512]{1,0:T(4,128)} %param.18) | copy-start | bytes 24580
  7.2 181.3 %all-reduce.84.cloned.1.call-start = ((), (), s32[]{:S(2)}) async-start(), calls=%async_computation | async-start | bytes 262144 | tf_op jit(solution)/shard_map/psum | solution.py:151
  8.4 15.8 %collective-permute-start.1 = (bf16[4,64,256]{2,1,0:T(8,128)(2,1)S(1)}, bf16[4,64,256]{2,1,0:T(8,128)(2,1)S(1)}, u32[]{:S(2)}, u32[]{:S(2)}) collective-permute-start(bf16[4,64,256]{2,1,0:T(8,128)(2,1)S(1)} %get-tuple-element.109), channel_id=1, source_target_pairs={{1,0},{2,1},{3,2},{4,3},{5,4},{6,5},{7,6},{8,7},{9,8},{10,9},{11,1... | collective-permute-start | bytes 393224 | tf_op jit(solution)/shard_map/ppermute | solution.py:19
  10.3 13.8 %collective-permute-start = (bf16[4,64,256]{2,1,0:T(8,128)(2,1)S(1)}, bf16[4,64,256]{2,1,0:T(8,128)(2,1)S(1)}, u32[]{:S(2)}, u32[]{:S(2)}) collective-permute-start(bf16[4,64,256]{2,1,0:T(8,128)(2,1)S(1)} %get-tuple-element.110), channel_id=1, source_target_pairs={{0,1},{1,2},{2,3},{3,4},{4,5},{5,6},{6,7},{7,8},{8,9},{9,10},{10,1... | collective-permute-start | bytes 393224 | tf_op jit(solution)/shard_map/ppermute | solution.py:16
  17.3 6.9 %copy-start.3 = (bf16[3,3,256,256]{3,2,1,0:T(8,128)(2,1)S(1)}, bf16[3,3,256,256]{3,2,1,0:T(8,128)(2,1)}, u32[]{:S(2)}) copy-start(bf16[3,3,256,256]{3,2,1,0:T(8,128)(2,1)} %param.14) | copy-start | bytes 3538948
  24.2 1.6 copy-start.2
  26.9 10.1 %collective-permute-start.2 = (bf16[4,64,256]{2,1,0:T(8,128)(2,1)S(1)}, bf16[4,64,256]{2,1,0:T(8,128)(2,1)S(1)}, u32[]{:S(2)}, u32[]{:S(2)}) collective-permute-start(bf16[4,64,256]{2,1,0:T(8,128)(2,1)S(1)} %get-tuple-element.107), channel_id=1, source_target_pairs={{0,1},{1,2},{2,3},{3,4},{4,5},{5,6},{6,7},{7,8},{8,9},{9,10},{10,1... | collective-permute-start | bytes 393224 | tf_op jit(solution)/shard_map/ppermute | solution.py:16
  30.0 8.8 %collective-permute-start.3 = (bf16[4,64,256]{2,1,0:T(8,128)(2,1)S(1)}, bf16[4,64,256]{2,1,0:T(8,128)(2,1)S(1)}, u32[]{:S(2)}, u32[]{:S(2)}) collective-permute-start(bf16[4,64,256]{2,1,0:T(8,128)(2,1)S(1)} %get-tuple-element.108), channel_id=1, source_target_pairs={{1,0},{2,1},{3,2},{4,3},{5,4},{6,5},{7,6},{8,7},{9,8},{10,9},{11,1... | collective-permute-start | bytes 393224 | tf_op jit(solution)/shard_map/ppermute | solution.py:19
  40.5 6.4 %collective-permute-start.4 = (bf16[4,64,256]{2,1,0:T(8,128)(2,1)S(1)}, bf16[4,64,256]{2,1,0:T(8,128)(2,1)S(1)}, u32[]{:S(2)}, u32[]{:S(2)}) collective-permute-start(bf16[4,64,256]{2,1,0:T(8,128)(2,1)S(1)} %get-tuple-element.105), channel_id=1, source_target_pairs={{0,1},{1,2},{2,3},{3,4},{4,5},{5,6},{6,7},{7,8},{8,9},{9,10},{10,1... | collective-permute-start | bytes 393224 | tf_op jit(solution)/shard_map/ppermute | solution.py:16
  42.4 6.3 %collective-permute-start.5 = (bf16[4,64,256]{2,1,0:T(8,128)(2,1)S(1)}, bf16[4,64,256]{2,1,0:T(8,128)(2,1)S(1)}, u32[]{:S(2)}, u32[]{:S(2)}) collective-permute-start(bf16[4,64,256]{2,1,0:T(8,128)(2,1)S(1)} %get-tuple-element.106), channel_id=1, source_target_pairs={{1,0},{2,1},{3,2},{4,3},{5,4},{6,5},{7,6},{8,7},{9,8},{10,9},{11,1... | collective-permute-start | bytes 393224 | tf_op jit(solution)/shard_map/ppermute | solution.py:19
  49.2 1.2 copy-start.4
  50.4 1.0 copy-start.5
  116.7 1.8 copy-start.6
  118.0 210.6 %all-reduce.86.cloned.1.call-start = ((), (), s32[]{:S(2)}) async-start(), calls=%async_computation.1 | async-start | bytes 262144 | tf_op jit(solution)/shard_map/psum | solution.py:152
  188.5 196.3 %all-reduce.88.cloned.1.call-start = ((), (), s32[]{:S(2)}) async-start(), calls=%async_computation.2 | async-start | bytes 262144 | tf_op jit(solution)/shard_map/psum | solution.py:153
Sparse Core Ops, SparseCore 0:
  118.1 70.3 all-reduce.83
  190.8 137.6 all-reduce.85
  330.8 53.8 all-reduce.87
where the time goes:
time: 393 us
  waiting for transfers between devices  269 us (68%)
  blocking collectives  52.2 us (13%)
  between operations  20.5 us (5%)
  starting transfers between devices  19.7 us (5%)
  other arithmetic  14.9 us (4%)
  matrix products  10.2 us (3%)
  local copies, waits for them, and re-layouts  6.28 us (2%)
    psum x1, waiting for transfers between devices, per_device(): head_grad = lax.psum(head_grad, 'outer')  140 us
    psum x1, waiting for transfers between devices, per_device(): head_grad = lax.psum(grad_local, 'inner')  69.9 us
    psum x1, waiting for transfers between devices, per_device(): head_grad = lax.psum(head_grad, 'take')  55.2 us
    all_gather x2, blocking collectives, exclusive_in_group(): gathered = lax.all_gather(totals, axis)  52.2 us
    ppermute x3, starting transfers between devices, extended_2(): lax.ppermute(lax.slice_in_dim(block, 0, width, axis=dim), axis, backward)  12.2 us
    add x13, other arithmetic, combine(): new_c = a_two * a_two * c_one / denom + c_two  9.96 us
    dot_general x9, matrix products, conv_layer(): jnp.einsum('tfw,wv->tfv', piece, weights[tap], preferred_element_type=jnp...  8.6 us
  transfers between devices with their start and end apart: 9, of which 7 were waited for; matrix products, arithmetic and copies ran while one was open for 2% of the time, Pallas kernels for 0%

commit v1 on v0

--- a/solution.py
+++ b/solution.py
@@ -149,7 +149,7 @@
         "tfw,tfs->ws", hidden, head_cotangent, preferred_element_type=jnp.float32
     )
     head_grad = lax.psum(grad_local, "inner")
-    head_grad = lax.psum(head_grad, "outer")
+    head_grad = jnp.sum(lax.all_gather(head_grad, "outer"), axis=0)
     head_grad = lax.psum(head_grad, "take")
     return (final[1], head_grad)
 

time: 393 us -> 278 us (0.71)
  waiting for transfers between devices: 269 us -> 158 us
  blocking collectives: 52.2 us -> 44.6 us
    psum x1 -> x0, waiting for transfers between devices: 140 us -> none  [per_device(): head_grad = lax.psum(head_grad, 'outer')]
    all_gather x0 -> x1, waiting for transfers between devices: none -> 44 us  [per_device(): head_grad = jnp.sum(lax.all_gather(head_grad, 'outer'), axis=0)]
    psum x1, waiting for transfers between devices: 69.9 us -> 56.2 us  [per_device(): head_grad = lax.psum(grad_local, 'inner')]
    all_gather x2, blocking collectives: 52.2 us -> 44.6 us  [exclusive_in_group(): gathered = lax.all_gather(totals, axis)]
  transfers between devices with their start and end apart: 9 -> 9, of which waited for: 7 -> 7; matrix products, arithmetic and copies ran while one was open for 2% -> 8% of each run, Pallas kernels for 0% -> 0%
where the time goes in v1:
time: 278 us; the launch traced here: 277 us
  waiting for transfers between devices  158 us (57%)
  blocking collectives  44.6 us (16%)
  between operations  20.5 us (7%)
  starting transfers between devices  19.7 us (7%)
  other arithmetic  17.2 us (6%)
  matrix products  11.1 us (4%)
  local copies, waits for them, and re-layouts  6.28 us (2%)
    psum x1, waiting for transfers between devices, per_device(): head_grad = lax.psum(grad_local, 'inner')  56.2 us
    psum x1, waiting for transfers between devices, per_device(): head_grad = lax.psum(head_grad, 'take')  53.7 us
    all_gather x2, blocking collectives, exclusive_in_group(): gathered = lax.all_gather(totals, axis)  44.6 us
    all_gather x1, waiting for transfers between devices, per_device(): head_grad = jnp.sum(lax.all_gather(head_grad, 'outer'), axis=0)  44 us
    ppermute x3, starting transfers between devices, extended_2(): lax.ppermute(lax.slice_in_dim(block, 0, width, axis=dim), axis, backward)  12 us
    add x13, other arithmetic, combine(): new_c = a_two * a_two * c_one / denom + c_two  9.73 us
    dot_general x9, matrix products, conv_layer(): jnp.einsum('tfw,wv->tfv', piece, weights[tap], preferred_element_type=jnp...  9.48 us
    ppermute x3, starting transfers between devices, extended_2(): lax.ppermute(lax.slice_in_dim(block, block.shape[dim] - width, None, axis...  7.34 us
  transfers between devices with their start and end apart: 9, of which 7 were waited for; matrix products, arithmetic and copies ran while one was open for 8% of the time, Pallas kernels for 0%

profile of v1, /device:TPU:2, one launch (start us, length us, event | category | flops | bytes accessed | tf_op | source)
XLA Modules:
  0.0 277.4 jit_solution(17072008989913779285)
XLA Ops:
  7.3 1.1 fusion.141
  8.4 1.9 collective-permute-start.1
  10.3 2.4 collective-permute-start
  12.7 0.8 exponential_bitcast_fusion
  13.5 0.8 fusion.142
  14.3 3.0 %fusion.60 = f32[4,512,256]{2,1,0:T(8,128)} fusion(bf16[4,512,256]{2,1,0:T(8,128)(2,1)} %param.13, bf16[3,3,256,256]{3,2,1,0:T(8,128)(2,1)} %param.14), kind=kOutput, calls=%fused_computation.134 | convolution fusion | flops 268435456 | bytes 3276800 | tf_op jit(solution)/shard_map/tfw,wv->tfv/dot_general | solution.py:105
  17.3 0.7 fusion.143
  24.2 0.5 fusion.16
  24.7 1.1 copy-done.2
  25.8 1.1 add_convert_fusion.2
  26.9 3.0 %collective-permute-start.2 = (bf16[4,64,256]{2,1,0:T(8,128)(2,1)S(1)}, bf16[4,64,256]{2,1,0:T(8,128)(2,1)S(1)}, u32[]{:S(2)}, u32[]{:S(2)}) collective-permute-start(bf16[4,64,256]{2,1,0:T(8,128)(2,1)S(1)} %get-tuple-element.107), channel_id=1, source_target_pairs={{0,1},{1,2},{2,3},{3,4},{4,5},{5,6},{6,7},{7,8},{8,9},{9,10},{10,1... | collective-permute-start | bytes 393224 | tf_op jit(solution)/shard_map/ppermute | solution.py:16
  30.0 6.3 %collective-permute-start.3 = (bf16[4,64,256]{2,1,0:T(8,128)(2,1)S(1)}, bf16[4,64,256]{2,1,0:T(8,128)(2,1)S(1)}, u32[]{:S(2)}, u32[]{:S(2)}) collective-permute-start(bf16[4,64,256]{2,1,0:T(8,128)(2,1)S(1)} %get-tuple-element.108), channel_id=1, source_target_pairs={{1,0},{2,1},{3,2},{4,3},{5,4},{6,5},{7,6},{8,7},{9,8},{10,9},{11,1... | collective-permute-start | bytes 393224 | tf_op jit(solution)/shard_map/ppermute | solution.py:19
  36.3 0.4 fusion.56
  36.7 0.3 collective-permute-done.2
  37.0 1.8 collective-permute-done.3
  38.9 0.4 fusion.10
  39.3 1.1 add_convert_fusion.1
  40.5 1.9 collective-permute-start.4
  42.4 3.8 %collective-permute-start.5 = (bf16[4,64,256]{2,1,0:T(8,128)(2,1)S(1)}, bf16[4,64,256]{2,1,0:T(8,128)(2,1)S(1)}, u32[]{:S(2)}, u32[]{:S(2)}) collective-permute-start(bf16[4,64,256]{2,1,0:T(8,128)(2,1)S(1)} %get-tuple-element.106), channel_id=1, source_target_pairs={{1,0},{2,1},{3,2},{4,3},{5,4},{6,5},{7,6},{8,7},{9,8},{10,9},{11,1... | collective-permute-start | bytes 393224 | tf_op jit(solution)/shard_map/ppermute | solution.py:19
  46.2 0.4 fusion.52
  46.6 0.3 collective-permute-done.4
  46.9 1.8 collective-permute-done.5
  48.8 0.4 fusion.4
  49.2 2.0 add_convert_fusion
  51.3 1.1 convolution_bitcast_fusion.1
  52.4 0.5 convolution_bitcast_fusion
  53.1 0.4 divide_select_fusion.1
  53.6 0.8 divide_add_fusion.14
  54.4 1.1 divide_add_fusion.13
  55.6 1.3 divide_add_fusion.12
  56.9 1.3 divide_add_fusion.11
  58.2 1.3 divide_add_fusion.10
  59.5 1.3 divide_add_fusion.9
  60.8 1.3 divide_add_fusion.8
  62.1 1.2 fusion.30
  63.4 0.7 fusion.31
  64.2 0.4 fusion.34
  64.7 0.5 fusion.38
  65.4 0.4 fusion.50
  65.8 0.3 slice_reduce_fusion
  66.1 13.5 %all-gather = f32[40,4,64]{2,1,0:T(4,128)S(1)} all-gather(f32[5,4,64]{2,1,0:T(4,128)S(1)} %constant_dynamic-update-slice_fusion.3), channel_id=2, replica_groups=mesh['take'=4,'outer'=16,'inner'=8] {'inner'}, dimensions={0}, use_global_device_ids=true | all-gather | bytes 46080 | tf_op jit(solution)/shard_map/all_gather | solution.py:69
  79.8 56.2 %all-reduce.83.cloned.1.call-done = f32[1,256,128]{2,1,0:T(8,128)} async-done(((f32[1,256,128]{2,1,0:T(8,128)}), f32[1,256,128]{2,1,0:T(8,128)}) %all-reduce.83.cloned.1.call-update) | async-done | bytes 131088 | tf_op jit(solution)/shard_map/psum | solution.py:151
  136.3 31.1 %all_gather.17 = f32[16,5,4,64]{3,2,0,1:T(4,128)S(1)} all-gather(f32[1,5,4,64]{3,2,0,1:T(4,128)S(1)} %slice.674), channel_id=1, replica_groups=mesh['take'=4,'outer'=16,'inner'=8] {'outer'}, dimensions={0}, use_global_device_ids=true | all-gather | bytes 87040 | tf_op jit(solution)/shard_map/all_gather | solution.py:69
  168.2 44.0 %all-gather.3.cloned.1.call-done = f32[16,256,128]{2,1,0:T(8,128)} async-done(((f32[1,256,128]{2,1,0:T(8,128)}), f32[16,256,128]{2,1,0:T(8,128)}) %all-gather.3.cloned.1.call-update) | async-done | bytes 2097168 | tf_op jit(solution)/shard_map/all_gather | solution.py:152
  212.2 2.4 reduce_sum.9
  214.6 1.0 divide_add_fusion
  215.6 53.7 %all-reduce.85.cloned.1.call-done = f32[256,128]{1,0:T(8,128)} async-done(((f32[256,128]{1,0:T(8,128)}), f32[256,128]{1,0:T(8,128)}) %all-reduce.85.cloned.1.call-update) | async-done | bytes 131088 | tf_op jit(solution)/shard_map/psum | solution.py:153
  269.3 1.6 copy.266
  (98 shorter events, 2.1 us)
Async XLA Ops:
  7.2 44.1 %copy-start = (bf16[4,512,128]{2,1,0:T(8,128)(2,1)S(1)}, bf16[4,512,128]{2,1,0:T(8,128)(2,1)}, u32[]{:S(2)}) copy-start(bf16[4,512,128]{2,1,0:T(8,128)(2,1)} %param.21) | copy-start | bytes 1572868
  7.2 16.9 %copy-start.1 = (bf16[4,512,256]{2,1,0:T(8,128)(2,1)S(1)}, bf16[4,512,256]{2,1,0:T(8,128)(2,1)}, u32[]{:S(2)}) copy-start(bf16[4,512,256]{2,1,0:T(8,128)(2,1)} %param.13) | copy-start | bytes 3145732
  7.2 10.1 %copy-start.8 = (s32[3]{0:T(128)S(1)}, s32[3]{0:T(128)}, u32[]{:S(2)}) copy-start(s32[3]{0:T(128)} %param.16) | copy-start | bytes 40
  7.2 16.8 %copy-start.7 = (s32[4,512]{1,0:T(4,128)S(1)}, s32[4,512]{1,0:T(4,128)}, u32[]{:S(2)}) copy-start(s32[4,512]{1,0:T(4,128)} %param.18) | copy-start | bytes 24580
  7.2 128.8 %all-reduce.83.cloned.1.call-start = ((), (), s32[]{:S(2)}) async-start(), calls=%async_computation | async-start | bytes 262144 | tf_op jit(solution)/shard_map/psum | solution.py:151
  8.4 15.8 %collective-permute-start.1 = (bf16[4,64,256]{2,1,0:T(8,128)(2,1)S(1)}, bf16[4,64,256]{2,1,0:T(8,128)(2,1)S(1)}, u32[]{:S(2)}, u32[]{:S(2)}) collective-permute-start(bf16[4,64,256]{2,1,0:T(8,128)(2,1)S(1)} %get-tuple-element.109), channel_id=1, source_target_pairs={{1,0},{2,1},{3,2},{4,3},{5,4},{6,5},{7,6},{8,7},{9,8},{10,9},{11,1... | collective-permute-start | bytes 393224 | tf_op jit(solution)/shard_map/ppermute | solution.py:19
  10.3 13.8 %collective-permute-start = (bf16[4,64,256]{2,1,0:T(8,128)(2,1)S(1)}, bf16[4,64,256]{2,1,0:T(8,128)(2,1)S(1)}, u32[]{:S(2)}, u32[]{:S(2)}) collective-permute-start(bf16[4,64,256]{2,1,0:T(8,128)(2,1)S(1)} %get-tuple-element.110), channel_id=1, source_target_pairs={{0,1},{1,2},{2,3},{3,4},{4,5},{5,6},{6,7},{7,8},{8,9},{9,10},{10,1... | collective-permute-start | bytes 393224 | tf_op jit(solution)/shard_map/ppermute | solution.py:16
  17.3 6.9 %copy-start.3 = (bf16[3,3,256,256]{3,2,1,0:T(8,128)(2,1)S(1)}, bf16[3,3,256,256]{3,2,1,0:T(8,128)(2,1)}, u32[]{:S(2)}) copy-start(bf16[3,3,256,256]{3,2,1,0:T(8,128)(2,1)} %param.14) | copy-start | bytes 3538948
  24.2 1.6 copy-start.2
  26.9 10.1 %collective-permute-start.2 = (bf16[4,64,256]{2,1,0:T(8,128)(2,1)S(1)}, bf16[4,64,256]{2,1,0:T(8,128)(2,1)S(1)}, u32[]{:S(2)}, u32[]{:S(2)}) collective-permute-start(bf16[4,64,256]{2,1,0:T(8,128)(2,1)S(1)} %get-tuple-element.107), channel_id=1, source_target_pairs={{0,1},{1,2},{2,3},{3,4},{4,5},{5,6},{6,7},{7,8},{8,9},{9,10},{10,1... | collective-permute-start | bytes 393224 | tf_op jit(solution)/shard_map/ppermute | solution.py:16
  30.0 8.8 %collective-permute-start.3 = (bf16[4,64,256]{2,1,0:T(8,128)(2,1)S(1)}, bf16[4,64,256]{2,1,0:T(8,128)(2,1)S(1)}, u32[]{:S(2)}, u32[]{:S(2)}) collective-permute-start(bf16[4,64,256]{2,1,0:T(8,128)(2,1)S(1)} %get-tuple-element.108), channel_id=1, source_target_pairs={{1,0},{2,1},{3,2},{4,3},{5,4},{6,5},{7,6},{8,7},{9,8},{10,9},{11,1... | collective-permute-start | bytes 393224 | tf_op jit(solution)/shard_map/ppermute | solution.py:19
  40.5 6.4 %collective-permute-start.4 = (bf16[4,64,256]{2,1,0:T(8,128)(2,1)S(1)}, bf16[4,64,256]{2,1,0:T(8,128)(2,1)S(1)}, u32[]{:S(2)}, u32[]{:S(2)}) collective-permute-start(bf16[4,64,256]{2,1,0:T(8,128)(2,1)S(1)} %get-tuple-element.105), channel_id=1, source_target_pairs={{0,1},{1,2},{2,3},{3,4},{4,5},{5,6},{6,7},{7,8},{8,9},{9,10},{10,1... | collective-permute-start | bytes 393224 | tf_op jit(solution)/shard_map/ppermute | solution.py:16
  42.4 6.3 %collective-permute-start.5 = (bf16[4,64,256]{2,1,0:T(8,128)(2,1)S(1)}, bf16[4,64,256]{2,1,0:T(8,128)(2,1)S(1)}, u32[]{:S(2)}, u32[]{:S(2)}) collective-permute-start(bf16[4,64,256]{2,1,0:T(8,128)(2,1)S(1)} %get-tuple-element.106), channel_id=1, source_target_pairs={{1,0},{2,1},{3,2},{4,3},{5,4},{6,5},{7,6},{8,7},{9,8},{10,9},{11,1... | collective-permute-start | bytes 393224 | tf_op jit(solution)/shard_map/ppermute | solution.py:19
  49.2 3.2 %copy-start.4 = (bf16[256,128]{1,0:T(8,128)(2,1)S(1)}, bf16[256,128]{1,0:T(8,128)(2,1)}, u32[]{:S(2)}) copy-start(bf16[256,128]{1,0:T(8,128)(2,1)} %param.17) | copy-start | bytes 196612
  52.4 1.2 copy-start.5
  52.9 159.3 %all-gather.3.cloned.1.call-start = ((), (), s32[]{:S(2)}) async-start(), calls=%async_computation.1 | async-start | bytes 2228224 | tf_op jit(solution)/shard_map/all_gather | solution.py:152
  136.0 133.3 %all-reduce.85.cloned.1.call-start = ((), (), s32[]{:S(2)}) async-start(), calls=%async_computation.2 | async-start | bytes 262144 | tf_op jit(solution)/shard_map/psum | solution.py:153
  136.2 32.0 %copy-start.6 = (f32[1,5,4,64]{3,2,1,0:T(4,128)S(1)}, f32[1,5,4,64]{3,2,1,0:T(4,128)}, u32[]{:S(2)}) copy-start(f32[1,5,4,64]{3,2,1,0:T(4,128)} %constant.139.clone.1) | copy-start | bytes 15364
Sparse Core Ops, SparseCore 0:
  53.0 82.9 all-reduce.82
  138.1 74.0 all-gather.2
  215.1 54.2 all-reduce.84
